TPU v7x, 32 devices: a whole 2x2x4 slice. The times are simulated.
32 devices in a mesh: gx: 4 (over x, core), gy: 8 (over z, y).
Axes of the slice: x: 2, y: 2, z: 4, core: 2. Of those that a mesh axis runs over, the one named last changes fastest.
Arguments:
- flow_state: float32 [6, 128, 16384], P(None, 'gx', 'gy'), may hold values from -6 to 6
- drag_coefficient: float32 [128, 16384], P('gx', 'gy'), may hold values from 0.05 to 0.5
- wet_mask: int32 [128, 16384], P('gx', 'gy'), may hold values 0 or 1
- target_elem: int32 [128, 16384], P('gx', 'gy'), may hold values from 0 to 8191, as said below
- target_node: int32 [128, 16384], P('gx', 'gy'), may hold values from 0 to 24
- displacement: float32 [3, 5, 5, 5, 2, 8, 1024], P(None, None, None, None, None, 'gx', 'gy'), as said below
- previous: float32 [3, 5, 5, 5, 2, 8, 1024], P(None, None, None, None, None, 'gx', 'gy'), as said below
- density: float32 [2, 8, 1024], P(None, 'gx', 'gy'), may hold values from 1 to 3
- lame_first: float32 [2, 8, 1024], P(None, 'gx', 'gy'), may hold values from 1 to 4
- shear_modulus: float32 [2, 8, 1024], P(None, 'gx', 'gy'), may hold values from 0.5 to 2
Outputs:
- flow_final: float32 [6, 128, 16384], P(None, 'gx', 'gy')
- displacement_next: float32 [3, 5, 5, 5, 2, 8, 1024], P(None, None, None, None, None, 'gx', 'gy')
- displacement_last: float32 [3, 5, 5, 5, 2, 8, 1024], P(None, None, None, None, None, 'gx', 'gy')
Inputs may be any that keep to these rules, and one draw needn't show every extreme that they name: `target_elem`: each cell's element lies at most one element row and one element column outside the 2 x 128 block of elements that shares the cell's device; the value is element row times 1024 plus element column. `displacement`: a grid point shared by adjacent elements holds the same value in every copy. `previous`: a grid point shared by adjacent elements holds the same value in every copy.
All inputs are finite; a program needn't handle non-finite values. No bound on the sum of `wet_mask` on one device may be relied on, other than what follows from the above.
Results may differ from a plain program's by a relative error of at most 0.00021.
Values sent between devices are 32-bit elements; how exact they have to be, the bound alone decides.
No kernel may reach another device: no remote copies, remote signals or barrier semaphores. Data moves between devices by JAX's collectives and lax.ppermute only.
A program may use at most 192 MiB of HBM per device.

v0:
```python
import jax
import jax.numpy as jnp
import numpy as np
from jax import lax
from jax.experimental import pallas as pl
from jax.experimental.pallas import tpu as pltpu
from jax.sharding import PartitionSpec as P

FLOW_STEPS = 4
SOLID_STEPS = 2


gll_points = np.array([-1.0, -np.sqrt(3.0 / 7.0), 0.0, np.sqrt(3.0 / 7.0), 1.0])
gll_weights = np.array([0.1, 49.0 / 90.0, 32.0 / 45.0, 49.0 / 90.0, 0.1])
flow_dt = 0.4
diffusion = 0.2
coupling = 0.5
upper_gravity = 0.8
density_ratio = 0.7
speed_floor = 0.0001
load_factor = 4.0
solid_dt = 0.04

ROW_PAD = 24
CHUNK = 1024
ROW_BLOCK = 8


def extended(block, sides, width):
    for axis, dim in sides:
        count = lax.axis_size(axis)
        forward = [(i, i + 1) for i in range(count - 1)]
        backward = [(target, source) for source, target in forward]
        low = lax.ppermute(
            lax.slice_in_dim(block, block.shape[dim] - width, None, axis=dim), axis, forward
        )
        high = lax.ppermute(lax.slice_in_dim(block, 0, width, axis=dim), axis, backward)
        block = jnp.concatenate([low, block, high], axis=dim)
    return block


def legendre_four(x):
    return (35.0 * x**4 - 30.0 * x**2 + 3.0) / 8.0


def derivative_table():
    result = np.zeros((5, 5))
    for i in range(5):
        for j in range(5):
            if i != j:
                result[i, j] = (
                    legendre_four(gll_points[i])
                    / legendre_four(gll_points[j])
                    / (gll_points[i] - gll_points[j])
                )
    result[0, 0] = -5.0
    result[4, 4] = 5.0
    return result


TABLE = derivative_table().astype(np.float32)


def pressures(fields, buoyancy):
    press_one = buoyancy * (fields[0] + fields[1])
    press_two = upper_gravity * (density_ratio * fields[0] + fields[1])
    return jnp.concatenate([fields, press_one[None], press_two[None]], axis=0)


def advance(center, padded, drag_coefficient):
    ahead_x = padded[:, 2:, 1:-1]
    behind_x = padded[:, :-2, 1:-1]
    ahead_y = padded[:, 1:-1, 2:]
    behind_y = padded[:, 1:-1, :-2]
    slope_x = 0.5 * (ahead_x - behind_x)
    slope_y = 0.5 * (ahead_y - behind_y)
    spread = ahead_x + behind_x + ahead_y + behind_y - 4.0 * center
    flow_speed = jnp.sqrt(center[2] * center[2] + center[3] * center[3] + speed_floor)
    dense_depth = center[0] - flow_dt * (slope_x[2] + slope_y[3]) + diffusion * spread[0]
    light_depth = center[1] - flow_dt * (slope_x[4] + slope_y[5]) + diffusion * spread[1]
    dense_xmom = (
        center[2]
        - flow_dt
        * (
            slope_x[6]
            + drag_coefficient * flow_speed * center[2]
            + coupling * (center[2] - center[4])
        )
        + diffusion * spread[2]
    )
    dense_ymom = (
        center[3]
        - flow_dt
        * (
            slope_y[6]
            + drag_coefficient * flow_speed * center[3]
            + coupling * (center[3] - center[5])
        )
        + diffusion * spread[3]
    )
    light_xmom = (
        center[4]
        - flow_dt * (slope_x[7] + coupling * (center[4] - center[2]))
        + diffusion * spread[4]
    )
    light_ymom = (
        center[5]
        - flow_dt * (slope_y[7] + coupling * (center[5] - center[3]))
        + diffusion * spread[5]
    )
    return jnp.stack([dense_depth, light_depth, dense_xmom, dense_ymom, light_xmom, light_ymom])


def basal_traction(fields, buoyancy, drag_coefficient):
    flow_speed = jnp.sqrt(fields[2] * fields[2] + fields[3] * fields[3] + speed_floor)
    press_one = buoyancy * (fields[0] + fields[1])
    rubbing = load_factor * drag_coefficient * flow_speed
    return jnp.stack([rubbing * fields[2], rubbing * fields[3], -load_factor * press_one])


def weights_cube():
    cube = (
        gll_weights.reshape(5, 1, 1) * gll_weights.reshape(1, 5, 1) * gll_weights.reshape(1, 1, 5)
    )
    return jnp.asarray(cube.reshape(5, 5, 5, 1, 1, 1), jnp.float32)


def load_kernel(trac_ref, row_ref, col_ref, out_ref):
    slots = out_ref.shape[0]

    @pl.when(pl.program_id(0) == 0)
    def _():
        out_ref[...] = jnp.zeros(out_ref.shape, out_ref.dtype)

    def row_body(r, carry):
        for c0 in range(0, row_ref.shape[1], CHUNK):
            point_row = row_ref[pl.ds(r, 1), pl.ds(c0, CHUNK)]
            point_col = col_ref[pl.ds(r, 1), pl.ds(c0, CHUNK)]
            hit = lax.broadcasted_iota(jnp.int32, (ROW_PAD, CHUNK), 0) == point_row
            pieces = []
            for k in range(3):
                value = trac_ref[k, pl.ds(r, 1), pl.ds(c0, CHUNK)]
                high = value.astype(jnp.bfloat16).astype(jnp.float32)
                low = value - high
                pieces.append(jnp.where(hit, high, 0.0))
                pieces.append(jnp.where(hit, low, 0.0))
            weighted = jnp.concatenate(pieces, axis=0).astype(jnp.bfloat16)
            onehot = (
                lax.broadcasted_iota(jnp.int32, (slots, CHUNK), 0) == point_col
            ).astype(jnp.bfloat16)
            out_ref[...] += lax.dot_general(
                onehot,
                weighted,
                (((1,), (1,)), ((), ())),
                preferred_element_type=jnp.float32,
            )
        return carry

    lax.fori_loop(0, ROW_BLOCK, row_body, 0)


def load_table(trac, point_row, point_col, slots):
    rows, cols = point_row.shape
    return pl.pallas_call(
        load_kernel,
        grid=(rows // ROW_BLOCK,),
        in_specs=[
            pl.BlockSpec((3, ROW_BLOCK, cols), lambda g: (0, g, 0)),
            pl.BlockSpec((ROW_BLOCK, cols), lambda g: (g, 0)),
            pl.BlockSpec((ROW_BLOCK, cols), lambda g: (g, 0)),
        ],
        out_specs=pl.BlockSpec((slots, 6 * ROW_PAD), lambda g: (0, 0)),
        out_shape=jax.ShapeDtypeStruct((slots, 6 * ROW_PAD), jnp.float32),
        compiler_params=pltpu.CompilerParams(dimension_semantics=("arbitrary",)),
    )(trac, point_row, point_col)


def along(x, axis, transpose):
    table = TABLE.T if transpose else TABLE
    shape = [1] * (x.ndim + 1)
    shape[axis] = 5
    shape[axis + 1] = 5
    coefs = jnp.asarray(table.reshape(shape))
    return jnp.sum(coefs * jnp.expand_dims(x, axis), axis=axis + 1)


def internal_force(values, lame_first, shear_modulus):
    weights_3d = weights_cube()
    gradients = [[along(values[i], j, False) for i in range(3)] for j in range(3)]
    divergence = gradients[0][0] + gradients[1][1] + gradients[2][2]
    forces = []
    for i in range(3):
        pulled = None
        for j in range(3):
            stress = shear_modulus * (gradients[j][i] + gradients[i][j])
            if i == j:
                stress = stress + lame_first * divergence
            term = along(weights_3d * stress, j, True)
            pulled = term if pulled is None else pulled + term
        forces.append(-pulled)
    return jnp.stack(forces)


def shift_block(block, axis, forward):
    count = lax.axis_size(axis)
    pairs = [(i, i + 1) for i in range(count - 1)]
    if not forward:
        pairs = [(target, source) for source, target in pairs]
    return lax.ppermute(block, axis, pairs)


def shift_faces(low_face, high_face, dim, axis):
    count = lax.axis_size(axis)
    forward = [(i, i + 1) for i in range(count - 1)]
    backward = [(target, source) for source, target in forward]
    size = low_face.shape[dim]
    from_prev = lax.ppermute(lax.slice_in_dim(high_face, size - 1, size, axis=dim), axis, forward)
    from_next = lax.ppermute(lax.slice_in_dim(low_face, 0, 1, axis=dim), axis, backward)
    before = jnp.concatenate([from_prev, lax.slice_in_dim(high_face, 0, size - 1, axis=dim)], axis=dim)
    after = jnp.concatenate([lax.slice_in_dim(low_face, 1, size, axis=dim), from_next], axis=dim)
    return before, after


def assemble_dim(values, node_dim, elem_dim, axis):
    low_face = lax.index_in_dim(values, 0, node_dim, keepdims=False)
    high_face = lax.index_in_dim(values, 4, node_dim, keepdims=False)
    face_elem_dim = elem_dim - 1
    if axis is None:
        size = low_face.shape[face_elem_dim]
        zero = jnp.zeros_like(lax.slice_in_dim(low_face, 0, 1, axis=face_elem_dim))
        before = jnp.concatenate(
            [zero, lax.slice_in_dim(high_face, 0, size - 1, axis=face_elem_dim)], axis=face_elem_dim
        )
        after = jnp.concatenate(
            [lax.slice_in_dim(low_face, 1, size, axis=face_elem_dim), zero], axis=face_elem_dim
        )
    else:
        before, after = shift_faces(low_face, high_face, face_elem_dim, axis)
    new_low = jnp.expand_dims(low_face + before, node_dim)
    new_high = jnp.expand_dims(high_face + after, node_dim)
    middle = lax.slice_in_dim(values, 1, 4, axis=node_dim)
    return jnp.concatenate([new_low, middle, new_high], axis=node_dim)


def assemble(values):
    values = assemble_dim(values, 1, 5, "gx")
    values = assemble_dim(values, 2, 6, "gy")
    values = assemble_dim(values, 3, 4, None)
    return values


def per_device(
    flow_state,
    drag_coefficient,
    wet_mask,
    target_elem,
    target_node,
    displacement,
    previous,
    density,
    lame_first,
    shear_modulus,
):
    buoyancy = 1.0 - 0.6 * wet_mask.astype(jnp.float32)
    fields = flow_state
    depth = FLOW_STEPS
    cell_rows = fields.shape[1]
    cell_cols = fields.shape[2]
    bundle = jnp.concatenate([fields, buoyancy[None], drag_coefficient[None]], axis=0)
    widened = extended(bundle, (("gx", 1), ("gy", 2)), depth)
    row_ids = lax.axis_index("gx") * cell_rows + jnp.arange(cell_rows + 2 * depth) - depth
    col_ids = lax.axis_index("gy") * cell_cols + jnp.arange(cell_cols + 2 * depth) - depth
    row_inside = (row_ids >= 0) & (row_ids < cell_rows * lax.axis_size("gx"))
    col_inside = (col_ids >= 0) & (col_ids < cell_cols * lax.axis_size("gy"))
    inside = (row_inside[:, None] & col_inside[None, :]).astype(jnp.float32)
    wide_fields = widened[:6]
    wide_buoyancy = widened[6]
    wide_drag = widened[7]
    for counter in range(FLOW_STEPS):
        stacked = pressures(wide_fields, wide_buoyancy)
        padded = jnp.pad(stacked, ((0, 0), (1, 1), (1, 1)))
        wide_fields = advance(stacked, padded, wide_drag) * inside[None]
    fields = wide_fields[:, depth : depth + cell_rows, depth : depth + cell_cols]
    traction = basal_traction(fields, buoyancy, drag_coefficient)
    block_rows = displacement.shape[5]
    block_cols = displacement.shape[6]
    devices_y = lax.axis_size("gy")
    surface_cols = block_cols * devices_y
    elem_row = target_elem // surface_cols
    elem_col = target_elem % surface_cols
    local_x = elem_row - block_rows * lax.axis_index("gx") + 1
    local_y = elem_col - block_cols * lax.axis_index("gy") + 1
    point_rows = 4 * (block_rows + 2) + 1
    point_cols = 4 * (block_cols + 2) + 1
    span_x = 4 * block_rows
    span_y = 4 * block_cols
    point_row = 4 * local_x + target_node // 5
    point_col = 4 * local_y + target_node % 5
    slots = -(-point_cols // 16) * 16
    grid = load_table(traction, point_row, point_col, slots)
    grid = grid.reshape(slots, 3, 2, ROW_PAD)
    grid = grid[:, :, 0] + grid[:, :, 1]
    overlap_x = point_rows - span_x
    overlap_y = point_cols - span_y
    from_next = shift_block(grid[:, :, :overlap_x], "gx", False)
    from_prev = shift_block(grid[:, :, span_x:point_rows], "gx", True)
    grid = (
        grid
        + jnp.pad(from_next, ((0, 0), (0, 0), (span_x, ROW_PAD - point_rows)))
        + jnp.pad(from_prev, ((0, 0), (0, 0), (0, ROW_PAD - overlap_x)))
    )
    from_next = shift_block(grid[:overlap_y], "gy", False)
    from_prev = shift_block(grid[span_y:point_cols], "gy", True)
    grid = (
        grid
        + jnp.pad(from_next, ((span_y, slots - point_cols), (0, 0), (0, 0)))
        + jnp.pad(from_prev, ((0, slots - overlap_y), (0, 0), (0, 0)))
    )
    by_col = jnp.concatenate(
        [
            grid[4 : 4 + span_y].reshape(block_cols, 4, 3, ROW_PAD),
            grid[8 : 8 + span_y].reshape(block_cols, 4, 3, ROW_PAD)[:, 0:1],
        ],
        axis=1,
    )
    by_row = jnp.concatenate(
        [
            by_col[..., 4 : 4 + span_x].reshape(block_cols, 5, 3, block_rows, 4),
            by_col[..., 8 : 8 + span_x].reshape(block_cols, 5, 3, block_rows, 4)[..., 0:1],
        ],
        axis=-1,
    )
    surface_load = jnp.transpose(by_row, (2, 4, 1, 3, 0))
    surface_load = surface_load.reshape(3, 5, 5, 1, 1, block_rows, block_cols)
    layers = displacement.shape[4]
    load_padded = jnp.pad(
        surface_load,
        ((0, 0), (0, 0), (0, 0), (0, 4), (0, layers - 1), (0, 0), (0, 0)),
    )
    masses = assemble(density[None, None, None, None] * weights_cube()[None])
    current = displacement
    for counter in range(SOLID_STEPS):
        force = assemble(internal_force(current, lame_first, shear_modulus)) + load_padded
        acceleration = force / masses
        advanced = 2.0 * current - previous + solid_dt * solid_dt * acceleration
        previous = current
        current = advanced
    return (fields, current, previous)


def solution(mesh):
    return jax.shard_map(
        per_device,
        mesh=mesh,
        in_specs=(
            P(None, "gx", "gy"),
            P("gx", "gy"),
            P("gx", "gy"),
            P("gx", "gy"),
            P("gx", "gy"),
            P(None, None, None, None, None, "gx", "gy"),
            P(None, None, None, None, None, "gx", "gy"),
            P(None, "gx", "gy"),
            P(None, "gx", "gy"),
            P(None, "gx", "gy"),
        ),
        out_specs=(
            P(None, "gx", "gy"),
            P(None, None, None, None, None, "gx", "gy"),
            P(None, None, None, None, None, "gx", "gy"),
        ),
        check_vma=False,
    )
```

profile of v0, /device:TPU:10, one launch (start us, length us, event | category | flops | bytes accessed | tf_op | source)
XLA Modules:
  0.0 242.9 jit_solution(10001524959745038224)
XLA Ops:
  1.7 2.2 pad_maximum_fusion.12
  3.9 1.9 collective-permute-start.1
  5.8 3.1 %collective-permute-start = (f32[8,4,2048]{2,1,0:T(4,128)}, f32[8,4,2048]{2,1,0:T(4,128)}, u32[]{:S(2)}, u32[]{:S(2)}) collective-permute-start(f32[8,4,2048]{2,1,0:T(4,128)} %get-tuple-element.89), channel_id=1, source_target_pairs={{0,8},{8,16},{16,24},{1,9},{9,17},{17,25},{2,10},{10,18},{18,26},{... | collective-permute-start | bytes 786440 | tf_op jit(solution)/shard_map/ppermute | solution.py:34
  9.2 8.0 %multiply_reduce_fusion.30 = (f32[5,5,5,2,2,128]{5,4,3,2,1,0:T(2,128)S(1)}, f32[5,5,5,2,2,128]{5,4,3,2,1,0:T(2,128)S(1)}, f32[5,5,5,2,2,128]{5,4,3,2,1,0:T(2,128...) fusion(f32[5,5,5,2,2,128]{5,4,3,2,1,0:T(2,128)S(1)} %get-tuple-, ...), kind=kLoop, calls=%fused_computation.65 | loop fusion | flops 5184000 | bytes 3072100 | tf_op jit(solution)/shard_map/reduce_sum | solution.py:184
  18.3 8.2 %multiply_reduce_fusion.29 = (f32[5,5,5,2,2,128]{5,4,3,2,1,0:T(2,128)S(1)}, f32[5,5,5,2,2,128]{5,4,3,2,1,0:T(2,128)S(1)}, f32[5,5,5,2,2,128]{5,4,3,2,1,0:T(2,128...) fusion(f32[5,5,5,2,2,128]{5,4,3,2,1,0:T(2,128)S(1)} %get-tuple-, ...), kind=kLoop, calls=%fused_computation.64 | loop fusion | flops 5184000 | bytes 3840100 | tf_op jit(solution)/shard_map/reduce_sum | solution.py:184
  27.4 14.8 %collective-permute-start.5 = (f32[3,5,5,2,1,128]{5,3,2,1,0,4:T(2,128)S(1)}, f32[3,5,5,2,1,128]{5,3,2,1,0,4:T(2,128)S(1)}, u32[]{:S(2)}, u32[]{:S(2)}) collective-permute-start(f32[3,5,5,2,1,128]{5,3,2,1,0,4:T(2,128)S(1)} %get-tuple-element.135), channel_id=1, source_target_pairs={{8,0},{16,8},{24,16},{9,1},{17,9},{25,17},{10,2},{18,10},{26,18},{... | collective-permute-start | bytes 230408 | tf_op jit(solution)/shard_map/ppermute | solution.py:218
  42.4 1.9 collective-permute-start.12
  44.5 3.1 %collective-permute-done.12 = f32[1,5,5,2,1,128]{5,3,2,1,4,0:T(2,128)S(1)} collective-permute-done((f32[1,5,5,2,1,128]{5,3,2,1,4,0:T(2,128)S(1)}, f32[1,5,5,2,1,128]{5,3,2,1,4,0:T(2,128)S(1)}, u32[]{:S(2)}, u32[]{:S(2)}) %collective-permute-start.12) | collective-permute-done | bytes 25632 | tf_op jit(solution)/shard_map/ppermute | solution.py:217
  47.6 1.9 collective-permute-start.13
  51.3 3.4 %collective-permute-start.14 = (f32[1,5,5,2,2,1]{5,4,3,1,2,0:T(2,128)S(1)}, f32[1,5,5,2,2,1]{5,4,3,1,2,0:T(2,128)S(1)}, u32[]{:S(2)}, u32[]{:S(2)}) collective-permute-start(f32[1,5,5,2,2,1]{5,4,3,1,2,0:T(2,128)S(1)} %slice.950), channel_id=1, source_target_pairs={{0,1},{1,2},{2,3},{3,4},{4,5},{5,6},{6,7},{8,9},{9,10},{10,11},{11... | collective-permute-start | bytes 1208 | tf_op jit(solution)/shard_map/ppermute | solution.py:217
  55.5 2.8 %collective-permute-done.14 = f32[1,5,5,2,2,1]{5,4,3,1,2,0:T(2,128)S(1)} collective-permute-done((f32[1,5,5,2,2,1]{5,4,3,1,2,0:T(2,128)S(1)}, f32[1,5,5,2,2,1]{5,4,3,1,2,0:T(2,128)S(1)}, u32[]{:S(2)}, u32[]{:S(2)}) %collective-permute-start.14) | collective-permute-done | bytes 432 | tf_op jit(solution)/shard_map/ppermute | solution.py:217
  58.9 2.4 collective-permute-start.15
  61.5 3.5 %collective-permute-done.15 = f32[1,5,5,2,2,1]{5,4,3,1,2,0:T(2,128)S(1)} collective-permute-done((f32[1,5,5,2,2,1]{5,4,3,1,2,0:T(2,128)S(1)}, f32[1,5,5,2,2,1]{5,4,3,1,2,0:T(2,128)S(1)}, u32[]{:S(2)}, u32[]{:S(2)}) %collective-permute-start.15) | collective-permute-done | bytes 432 | tf_op jit(solution)/shard_map/ppermute | solution.py:218
  67.2 1.9 collective-permute-start.4
  69.7 3.1 %collective-permute-done.4 = f32[3,5,5,2,1,128]{5,3,2,1,0,4:T(2,128)S(1)} collective-permute-done((f32[3,5,5,2,1,128]{5,3,2,1,0,4:T(2,128)S(1)}, f32[3,5,5,2,1,128]{5,3,2,1,0,4:T(2,128)S(1)}, u32[]{:S(2)}, u32[]{:S(2)}) %collective-permute-start.4) | collective-permute-done | bytes 76832 | tf_op jit(solution)/shard_map/ppermute | solution.py:217
  74.4 3.3 %collective-permute-start.7 = (f32[3,5,5,2,2,1]{5,4,3,2,1,0:T(2,128)S(1)}, f32[3,5,5,2,2,1]{5,4,3,2,1,0:T(2,128)}, u32[]{:S(2)}, u32[]{:S(2)}) collective-permute-start(f32[3,5,5,2,2,1]{5,4,3,2,1,0:T(2,128)S(1)} %bitcast.196), channel_id=1, source_target_pairs={{1,0},{2,1},{3,2},{4,3},{5,4},{6,5},{7,6},{9,8},{10,9},{11,10},{12... | collective-permute-start | bytes 3608 | tf_op jit(solution)/shard_map/ppermute | solution.py:218
  79.5 2.5 %collective-permute-start.6 = (f32[3,5,5,2,2,1]{5,4,3,2,1,0:T(2,128)}, f32[3,5,5,2,2,1]{5,4,3,2,1,0:T(2,128)}, u32[]{:S(2)}, u32[]{:S(2)}) collective-permute-start(f32[3,5,5,2,2,1]{5,4,3,2,1,0:T(2,128)} %slice.922), channel_id=1, source_target_pairs={{0,1},{1,2},{2,3},{3,4},{4,5},{5,6},{6,7},{8,9},{9,10},{10,11},{11... | collective-permute-start | bytes 3608 | tf_op jit(solution)/shard_map/ppermute | solution.py:217
  84.5 1.9 maximum_add_fusion.3
  91.6 1.7 pad_maximum_fusion.4
  93.4 3.0 %collective-permute-start.2 = (f32[8,40,4]{2,1,0:T(8,128)S(1)}, f32[8,40,4]{2,1,0:T(8,128)S(1)}, u32[]{:S(2)}, u32[]{:S(2)}) collective-permute-start(f32[8,40,4]{2,1,0:T(8,128)S(1)} %get-tuple-element.86), channel_id=1, source_target_pairs={{0,1},{1,2},{2,3},{3,4},{4,5},{5,6},{6,7},{8,9},{9,10},{10,11},{11... | collective-permute-start | bytes 15368 | tf_op jit(solution)/shard_map/ppermute | solution.py:34
  96.3 3.8 %collective-permute-start.3 = (f32[8,40,4]{2,1,0:T(8,128)S(1)}, f32[8,40,4]{2,1,0:T(8,128)}, u32[]{:S(2)}, u32[]{:S(2)}) collective-permute-start(f32[8,40,4]{2,1,0:T(8,128)S(1)} %get-tuple-element.85), channel_id=1, source_target_pairs={{1,0},{2,1},{3,2},{4,3},{5,4},{6,5},{7,6},{9,8},{10,9},{11,10},{12... | collective-permute-start | bytes 15368 | tf_op jit(solution)/shard_map/ppermute | solution.py:37
  102.2 1.5 collective-permute-done.3
  103.7 3.2 %concatenate.178 = f32[8,40,2056]{2,1,0:T(8,128)S(1)} concatenate(f32[8,40,4]{2,1,0:T(8,128)} %copy-done.27, f32[8,40,2048]{2,1,0:T(8,128)} %copy-done, f32[8,40,4]{2,1,0:T(8,128)} %collective-permute-done.3), dimensions={2} | concatenate | bytes 5263360 | tf_op jit(solution)/shard_map/concatenate | solution.py:38
  107.3 3.6 %subtract_multiply_fusion.7 = (f32[8,40,2056]{2,1,0:T(8,128)S(1)}, f32[8,40,2056]{2,1,0:T(8,128)S(1)}, f32[8,40,2056]{2,1,0:T(8,128)S(1)}) fusion(f32[8,40,2056]{2,1,0:T(8,128)S(1)} %pad_maximum_fusion), kind=kLoop, calls=%fused_computation.31 | loop fusion | flops 5921280 | bytes 10526720 | tf_op jit(solution)/shard_map/mul | solution.py:75
  112.2 3.6 %subtract_multiply_fusion.5 = (f32[8,40,2056]{2,1,0:T(8,128)S(1)}, f32[8,40,2056]{2,1,0:T(8,128)S(1)}, f32[8,40,2056]{2,1,0:T(8,128)S(1)}) fusion(f32[8,40,2056]{2,1,0:T(8,128)S(1)} %pad_maximum_fusion.1), kind=kLoop, calls=%fused_computation.28 | loop fusion | flops 5921280 | bytes 10526720 | tf_op jit(solution)/shard_map/mul | solution.py:75
  117.3 3.6 %subtract_multiply_fusion.3 = (f32[8,40,2056]{2,1,0:T(8,128)S(1)}, f32[8,40,2056]{2,1,0:T(8,128)S(1)}, f32[8,40,2056]{2,1,0:T(8,128)S(1)}) fusion(f32[8,40,2056]{2,1,0:T(8,128)S(1)} %pad_maximum_fusion.2), kind=kLoop, calls=%fused_computation.25 | loop fusion | flops 5921280 | bytes 10526720 | tf_op jit(solution)/shard_map/mul | solution.py:75
  122.3 4.0 %subtract_multiply_fusion.1 = (f32[8,40,2056]{2,1,0:T(8,128)S(1)}, f32[8,40,2056]{2,1,0:T(8,128)S(1)}, f32[8,40,2056]{2,1,0:T(8,128)S(1)}) fusion(f32[8,40,2056]{2,1,0:T(8,128)S(1)} %pad_maximum_fusion.3), kind=kLoop, calls=%fused_computation.22 | loop fusion | flops 5921280 | bytes 10526720 | tf_op jit(solution)/shard_map/mul | solution.py:75
  129.6 27.6 %shard_map.472 = f32[528,144]{1,0:T(8,128)} custom-call(f32[3,32,2048]{2,1,0:T(8,128)} %pad_maximum_fusion.5.trac_ref, s32[32,2048]{1,0:T(8,128)} %get-tuple-element.116.row_ref, s32[32,2048]{1,0:T(8,128)} %get-tuple-element.115.col_ref), custom_call_target="tpu_custom_call" | custom-call | tf_op jit(solution)/shard_map/pallas_call | solution.py:164
  158.5 2.1 collective-permute-start.9
  160.6 3.6 %collective-permute-start.8 = (f32[528,3,9]{0,2,1:T(8,128)S(1)}, f32[528,3,9]{0,2,1:T(8,128)S(1)}, u32[]{:S(2)}, u32[]{:S(2)}) collective-permute-start(f32[528,3,9]{0,2,1:T(8,128)S(1)} %get-tuple-element.126), channel_id=1, source_target_pairs={{8,0},{16,8},{24,16},{9,1},{17,9},{25,17},{10,2},{18,10},{26,18},{... | collective-permute-start | bytes 171080 | tf_op jit(solution)/shard_map/ppermute | solution.py:209
  164.3 1.7 add_bitcast_fusion.3
  166.7 4.8 %collective-permute-start.11 = (f32[9,3,24]{0,2,1:T(8,128)S(1)}, f32[9,3,24]{0,2,1:T(8,128)S(1)}, u32[]{:S(2)}, u32[]{:S(2)}) collective-permute-start(f32[9,3,24]{0,2,1:T(8,128)S(1)} %get-tuple-element.125), channel_id=1, source_target_pairs={{0,1},{1,2},{2,3},{3,4},{4,5},{5,6},{6,7},{8,9},{9,10},{10,11},{11... | collective-permute-start | bytes 7784 | tf_op jit(solution)/shard_map/ppermute | solution.py:209
  171.5 1.9 collective-permute-start.10
  174.3 3.1 %collective-permute-done.10 = f32[9,3,24]{0,2,1:T(8,128)S(1)} collective-permute-done((f32[9,3,24]{0,2,1:T(8,128)S(1)}, f32[9,3,24]{0,2,1:T(8,128)S(1)}, u32[]{:S(2)}, u32[]{:S(2)}) %collective-permute-start.10) | collective-permute-done | bytes 2624 | tf_op jit(solution)/shard_map/ppermute | solution.py:209
  180.7 2.1 copy.255
  182.8 2.0 copy.257
  185.9 2.4 multiply_add_fusion.1
  189.5 7.8 %multiply_reduce_fusion.4 = (f32[5,5,5,2,2,128]{5,4,3,2,1,0:T(2,128)S(1)}, f32[5,5,5,2,2,128]{5,4,3,2,1,0:T(2,128)S(1)}, f32[5,5,5,2,2,128]{5,4,3,2,1,0:T(2,128)...) fusion(f32[5,5,5,2,2,128]{5,4,3,2,1,0:T(2,128)S(1)} %get-tuple-, ...), kind=kLoop, calls=%fused_computation.39 | loop fusion | flops 5184000 | bytes 3072100 | tf_op jit(solution)/shard_map/reduce_sum | solution.py:184
  198.2 8.3 %multiply_reduce_fusion.1 = (f32[5,5,5,2,2,128]{5,4,3,2,1,0:T(2,128)S(1)}, f32[5,5,5,2,2,128]{5,4,3,2,1,0:T(2,128)S(1)}, f32[5,5,5,2,2,128]{5,4,3,2,1,0:T(2,128)...) fusion(f32[5,5,5,2,2,128]{5,4,3,2,1,0:T(2,128)S(1)} %get-tuple-, ...), kind=kLoop, calls=%fused_computation.36 | loop fusion | flops 5184000 | bytes 3840100 | tf_op jit(solution)/shard_map/reduce_sum | solution.py:184
  207.9 1.9 collective-permute-start.16
  209.9 3.8 %collective-permute-done.16 = f32[3,5,5,2,1,128]{5,3,0,2,1,4:T(2,128)S(1)} collective-permute-done((f32[3,5,5,2,1,128]{5,3,0,2,1,4:T(2,128)S(1)}, f32[3,5,5,2,1,128]{5,3,0,2,1,4:T(2,128)S(1)}, u32[]{:S(2)}, u32[]{:S(2)}) %collective-permute-start.16) | collective-permute-done | bytes 76832 | tf_op jit(solution)/shard_map/ppermute | solution.py:217
  213.9 1.9 collective-permute-start.17
  216.0 1.6 slice.915
  218.7 3.0 %collective-permute-start.18 = (f32[3,5,5,2,2,1]{5,4,3,1,0,2:T(2,128)S(1)}, f32[3,5,5,2,2,1]{5,4,3,1,0,2:T(2,128)S(1)}, u32[]{:S(2)}, u32[]{:S(2)}) collective-permute-start(f32[3,5,5,2,2,1]{5,4,3,1,0,2:T(2,128)S(1)} %slice.966), channel_id=1, source_target_pairs={{0,1},{1,2},{2,3},{3,4},{4,5},{5,6},{6,7},{8,9},{9,10},{10,11},{11... | collective-permute-start | bytes 3608 | tf_op jit(solution)/shard_map/ppermute | solution.py:217
  221.8 6.0 %collective-permute-done.18 = f32[3,5,5,2,2,1]{5,4,3,1,0,2:T(2,128)S(1)} collective-permute-done((f32[3,5,5,2,2,1]{5,4,3,1,0,2:T(2,128)S(1)}, f32[3,5,5,2,2,1]{5,4,3,1,0,2:T(2,128)S(1)}, u32[]{:S(2)}, u32[]{:S(2)}) %collective-permute-start.18) | collective-permute-done | bytes 1232 | tf_op jit(solution)/shard_map/ppermute | solution.py:217
  229.1 2.1 collective-permute-start.19
  232.1 4.7 %collective-permute-done.19 = f32[3,5,5,2,2,1]{5,4,3,1,0,2:T(2,128)} collective-permute-done((f32[3,5,5,2,2,1]{5,4,3,1,0,2:T(2,128)S(1)}, f32[3,5,5,2,2,1]{5,4,3,1,0,2:T(2,128)}, u32[]{:S(2)}, u32[]{:S(2)}) %collective-permute-start.19) | collective-permute-done | bytes 1232 | tf_op jit(solution)/shard_map/ppermute | solution.py:218
  240.9 1.8 multiply_add_fusion
  (230 shorter events, 48.6 us)
Async XLA Ops:
  0.6 8.6 %copy-start.29 = (f32[5,5]{1,0:T(8,128)S(1)}, f32[5,5]{1,0:T(8,128)}, u32[]{:S(2)}) copy-start(f32[5,5]{1,0:T(8,128)} %constant.160) | copy-start | bytes 304
  0.6 8.3 %copy-start.3 = (f32[3,5,5,5,2,2,128]{6,5,4,3,2,1,0:T(2,128)S(1)}, f32[3,5,5,5,2,2,128]{6,5,4,3,2,1,0:T(2,128)}, u32[]{:S(2)}) copy-start(f32[3,5,5,5,2,2,128]{6,5,4,3,2,1,0:T(2,128)} %param.54) | copy-start | bytes 2304004
  1.7 4.1 %copy-start.13 = (f32[1,32,2048]{2,1,0:T(8,128)}, f32[1,32,2048]{2,1,0:T(8,128)S(1)}, u32[]{:S(2)}) copy-start(f32[1,32,2048]{2,1,0:T(8,128)S(1)} %fusion.127) | copy-start | bytes 786436
  3.9 87.6 %collective-permute-start.1 = (f32[8,4,2048]{2,1,0:T(4,128)}, f32[8,4,2048]{2,1,0:T(4,128)}, u32[]{:S(2)}, u32[]{:S(2)}) collective-permute-start(f32[8,4,2048]{2,1,0:T(4,128)} %get-tuple-element.90), channel_id=1, source_target_pairs={{8,0},{16,8},{24,16},{9,1},{17,9},{25,17},{10,2},{18,10},{26,18},{... | collective-permute-start | bytes 786440 | tf_op jit(solution)/shard_map/ppermute | solution.py:37
  5.8 85.7 %collective-permute-start = (f32[8,4,2048]{2,1,0:T(4,128)}, f32[8,4,2048]{2,1,0:T(4,128)}, u32[]{:S(2)}, u32[]{:S(2)}) collective-permute-start(f32[8,4,2048]{2,1,0:T(4,128)} %get-tuple-element.89), channel_id=1, source_target_pairs={{0,8},{8,16},{16,24},{1,9},{9,17},{17,25},{2,10},{10,18},{18,26},{... | collective-permute-start | bytes 786440 | tf_op jit(solution)/shard_map/ppermute | solution.py:34
  9.2 8.1 %copy-start.26 = (f32[5,5,5]{2,1,0:T(8,128)S(1)}, f32[5,5,5]{2,1,0:T(8,128)}, u32[]{:S(2)}) copy-start(f32[5,5,5]{2,1,0:T(8,128)} %constant.159) | copy-start | bytes 1504
  9.2 8.1 %copy-start.31 = (f32[2,2,128]{2,1,0:T(2,128)S(1)}, f32[2,2,128]{2,1,0:T(2,128)}, u32[]{:S(2)}) copy-start(f32[2,2,128]{2,1,0:T(2,128)} %param.58) | copy-start | bytes 6148
  9.2 8.1 %copy-start.33 = (f32[2,2,128]{2,1,0:T(2,128)S(1)}, f32[2,2,128]{2,1,0:T(2,128)}, u32[]{:S(2)}) copy-start(f32[2,2,128]{2,1,0:T(2,128)} %param.57) | copy-start | bytes 6148
  26.5 15.7 %copy-start.35 = (f32[2,2,128]{2,1,0:T(2,128)S(1)}, f32[2,2,128]{2,1,0:T(2,128)}, u32[]{:S(2)}) copy-start(f32[2,2,128]{2,1,0:T(2,128)} %param.56) | copy-start | bytes 6148
  26.7 22.8 %copy-start.24 = (s32[32,2048]{1,0:T(8,128)S(1)}, s32[32,2048]{1,0:T(8,128)}, u32[]{:S(2)}) copy-start(s32[32,2048]{1,0:T(8,128)} %param.53) | copy-start | bytes 786436
  26.8 22.8 %copy-start.25 = (s32[32,2048]{1,0:T(8,128)S(1)}, s32[32,2048]{1,0:T(8,128)}, u32[]{:S(2)}) copy-start(s32[32,2048]{1,0:T(8,128)} %param.52) | copy-start | bytes 786436
  27.4 39.5 %collective-permute-start.5 = (f32[3,5,5,2,1,128]{5,3,2,1,0,4:T(2,128)S(1)}, f32[3,5,5,2,1,128]{5,3,2,1,0,4:T(2,128)S(1)}, u32[]{:S(2)}, u32[]{:S(2)}) collective-permute-start(f32[3,5,5,2,1,128]{5,3,2,1,0,4:T(2,128)S(1)} %get-tuple-element.135), channel_id=1, source_target_pairs={{8,0},{16,8},{24,16},{9,1},{17,9},{25,17},{10,2},{18,10},{26,18},{... | collective-permute-start | bytes 230408 | tf_op jit(solution)/shard_map/ppermute | solution.py:218
  42.4 5.2 %collective-permute-start.12 = (f32[1,5,5,2,1,128]{5,3,2,1,4,0:T(2,128)S(1)}, f32[1,5,5,2,1,128]{5,3,2,1,4,0:T(2,128)S(1)}, u32[]{:S(2)}, u32[]{:S(2)}) collective-permute-start(f32[1,5,5,2,1,128]{5,3,2,1,4,0:T(2,128)S(1)} %get-tuple-element.136), channel_id=1, source_target_pairs={{0,8},{8,16},{16,24},{1,9},{9,17},{17,25},{2,10},{10,18},{18,26},{... | collective-permute-start | bytes 76808 | tf_op jit(solution)/shard_map/ppermute | solution.py:217
  47.6 3.5 %collective-permute-start.13 = (f32[1,5,5,2,1,128]{5,3,2,1,4,0:T(2,128)S(1)}, f32[1,5,5,2,1,128]{5,3,2,1,4,0:T(2,128)S(1)}, u32[]{:S(2)}, u32[]{:S(2)}) collective-permute-start(f32[1,5,5,2,1,128]{5,3,2,1,4,0:T(2,128)S(1)} %get-tuple-element.139), channel_id=1, source_target_pairs={{8,0},{16,8},{24,16},{9,1},{17,9},{25,17},{10,2},{18,10},{26,18},{... | collective-permute-start | bytes 76808 | tf_op jit(solution)/shard_map/ppermute | solution.py:218
  51.3 7.0 %collective-permute-start.14 = (f32[1,5,5,2,2,1]{5,4,3,1,2,0:T(2,128)S(1)}, f32[1,5,5,2,2,1]{5,4,3,1,2,0:T(2,128)S(1)}, u32[]{:S(2)}, u32[]{:S(2)}) collective-permute-start(f32[1,5,5,2,2,1]{5,4,3,1,2,0:T(2,128)S(1)} %slice.950), channel_id=1, source_target_pairs={{0,1},{1,2},{2,3},{3,4},{4,5},{5,6},{6,7},{8,9},{9,10},{10,11},{11... | collective-permute-start | bytes 1208 | tf_op jit(solution)/shard_map/ppermute | solution.py:217
  58.9 14.2 %copy-start.14 = (f32[1,5,1,5,2,2,128]{6,5,4,2,1,3,0:T(2,128)}, f32[1,5,1,5,2,2,128]{6,5,4,2,1,3,0:T(2,128)S(1)}, u32[]{:S(2)}) copy-start(f32[1,5,1,5,2,2,128]{6,5,4,2,1,3,0:T(2,128)S(1)} %get-tuple-element.65) | copy-start | bytes 153604
  58.9 6.0 %collective-permute-start.15 = (f32[1,5,5,2,2,1]{5,4,3,1,2,0:T(2,128)S(1)}, f32[1,5,5,2,2,1]{5,4,3,1,2,0:T(2,128)S(1)}, u32[]{:S(2)}, u32[]{:S(2)}) collective-permute-start(f32[1,5,5,2,2,1]{5,4,3,1,2,0:T(2,128)S(1)} %bitcast.204), channel_id=1, source_target_pairs={{1,0},{2,1},{3,2},{4,3},{5,4},{6,5},{7,6},{9,8},{10,9},{11,10},{12... | collective-permute-start | bytes 1208 | tf_op jit(solution)/shard_map/ppermute | solution.py:218
  67.2 5.7 %collective-permute-start.4 = (f32[3,5,5,2,1,128]{5,3,2,1,0,4:T(2,128)S(1)}, f32[3,5,5,2,1,128]{5,3,2,1,0,4:T(2,128)S(1)}, u32[]{:S(2)}, u32[]{:S(2)}) collective-permute-start(f32[3,5,5,2,1,128]{5,3,2,1,0,4:T(2,128)S(1)} %get-tuple-element.132), channel_id=1, source_target_pairs={{0,8},{8,16},{16,24},{1,9},{9,17},{17,25},{2,10},{10,18},{18,26},{... | collective-permute-start | bytes 230408 | tf_op jit(solution)/shard_map/ppermute | solution.py:217
  73.5 18.1 %copy-start.7 = (f32[6,32,2048]{2,1,0:T(8,128)S(1)}, f32[6,32,2048]{2,1,0:T(8,128)}, u32[]{:S(2)}) copy-start(f32[6,32,2048]{2,1,0:T(8,128)} %param.49) | copy-start | bytes 4718596
  74.4 7.6 %collective-permute-start.7 = (f32[3,5,5,2,2,1]{5,4,3,2,1,0:T(2,128)S(1)}, f32[3,5,5,2,2,1]{5,4,3,2,1,0:T(2,128)}, u32[]{:S(2)}, u32[]{:S(2)}) collective-permute-start(f32[3,5,5,2,2,1]{5,4,3,2,1,0:T(2,128)S(1)} %bitcast.196), channel_id=1, source_target_pairs={{1,0},{2,1},{3,2},{4,3},{5,4},{6,5},{7,6},{9,8},{10,9},{11,10},{12... | collective-permute-start | bytes 3608 | tf_op jit(solution)/shard_map/ppermute | solution.py:218
  78.6 21.6 %copy-start.1 = (f32[3,5,3,5,2,2,128]{6,5,4,3,2,1,0:T(2,128)}, f32[3,5,3,5,2,2,128]{6,5,4,3,2,1,0:T(2,128)S(1)}, u32[]{:S(2)}) copy-start(f32[3,5,3,5,2,2,128]{6,5,4,3,2,1,0:T(2,128)S(1)} %slice.924) | copy-start | bytes 1382404
  79.5 8.3 %collective-permute-start.6 = (f32[3,5,5,2,2,1]{5,4,3,2,1,0:T(2,128)}, f32[3,5,5,2,2,1]{5,4,3,2,1,0:T(2,128)}, u32[]{:S(2)}, u32[]{:S(2)}) collective-permute-start(f32[3,5,5,2,2,1]{5,4,3,2,1,0:T(2,128)} %slice.922), channel_id=1, source_target_pairs={{0,1},{1,2},{2,3},{3,4},{4,5},{5,6},{6,7},{8,9},{9,10},{10,11},{11... | collective-permute-start | bytes 3608 | tf_op jit(solution)/shard_map/ppermute | solution.py:217
  91.5 8.6 %copy-start.10 = (f32[3,5,1,5,2,2,128]{6,5,4,3,2,1,0:T(2,128)}, f32[3,5,1,5,2,2,128]{6,5,4,3,2,1,0:T(2,128)S(1)}, u32[]{:S(2)}) copy-start(f32[3,5,1,5,2,2,128]{6,5,4,3,2,1,0:T(2,128)S(1)} %fusion.130) | copy-start | bytes 460804
  91.5 8.6 %copy-start.8 = (f32[3,5,1,5,2,2,128]{6,5,4,3,2,1,0:T(2,128)S(1)}, f32[3,5,1,5,2,2,128]{6,5,4,3,2,1,0:T(2,128)}, u32[]{:S(2)}) copy-start(f32[3,5,1,5,2,2,128]{6,5,4,3,2,1,0:T(2,128)} %maximum_add_fusion.3) | copy-start | bytes 460804
  93.3 8.2 %copy-start = (f32[8,40,2048]{2,1,0:T(8,128)}, f32[8,40,2048]{2,1,0:T(8,128)S(1)}, u32[]{:S(2)}) copy-start(f32[8,40,2048]{2,1,0:T(8,128)S(1)} %pad_maximum_fusion.4) | copy-start | bytes 7864324
  93.4 8.1 %collective-permute-start.2 = (f32[8,40,4]{2,1,0:T(8,128)S(1)}, f32[8,40,4]{2,1,0:T(8,128)S(1)}, u32[]{:S(2)}, u32[]{:S(2)}) collective-permute-start(f32[8,40,4]{2,1,0:T(8,128)S(1)} %get-tuple-element.86), channel_id=1, source_target_pairs={{0,1},{1,2},{2,3},{3,4},{4,5},{5,6},{6,7},{8,9},{9,10},{10,11},{11... | collective-permute-start | bytes 15368 | tf_op jit(solution)/shard_map/ppermute | solution.py:34
  96.3 7.3 %collective-permute-start.3 = (f32[8,40,4]{2,1,0:T(8,128)S(1)}, f32[8,40,4]{2,1,0:T(8,128)}, u32[]{:S(2)}, u32[]{:S(2)}) collective-permute-start(f32[8,40,4]{2,1,0:T(8,128)S(1)} %get-tuple-element.85), channel_id=1, source_target_pairs={{1,0},{2,1},{3,2},{4,3},{5,4},{6,5},{7,6},{9,8},{10,9},{11,10},{12... | collective-permute-start | bytes 15368 | tf_op jit(solution)/shard_map/ppermute | solution.py:37
  128.7 35.6 %copy-start.2 = (f32[3,5,3,5,2,2,128]{6,5,4,3,2,1,0:T(2,128)S(1)}, f32[3,5,3,5,2,2,128]{6,5,4,3,2,1,0:T(2,128)}, u32[]{:S(2)}) copy-start(f32[3,5,3,5,2,2,128]{6,5,4,3,2,1,0:T(2,128)} %copy-done.1) | copy-start | bytes 1382404
  128.7 35.6 %copy-start.9 = (f32[3,5,1,5,2,2,128]{6,5,4,3,2,1,0:T(2,128)S(1)}, f32[3,5,1,5,2,2,128]{6,5,4,3,2,1,0:T(2,128)}, u32[]{:S(2)}) copy-start(f32[3,5,1,5,2,2,128]{6,5,4,3,2,1,0:T(2,128)} %maximum_add_fusion.3) | copy-start | bytes 460804
  128.7 35.6 %copy-start.11 = (f32[3,5,1,5,2,2,128]{6,5,4,3,2,1,0:T(2,128)S(1)}, f32[3,5,1,5,2,2,128]{6,5,4,3,2,1,0:T(2,128)}, u32[]{:S(2)}) copy-start(f32[3,5,1,5,2,2,128]{6,5,4,3,2,1,0:T(2,128)} %copy-done.10) | copy-start | bytes 460804
  158.5 15.0 %copy-start.20 = (f32[3,5,5,2,2,128]{5,4,3,2,1,0:T(2,128)S(1)}, f32[3,5,5,2,2,128]{5,4,3,2,1,0:T(2,128)}, u32[]{:S(2)}) copy-start(f32[3,5,5,2,2,128]{5,4,3,2,1,0:T(2,128)} %copy-done.19) | copy-start | bytes 460804
  158.5 7.4 %collective-permute-start.9 = (f32[528,3,9]{0,2,1:T(8,128)S(1)}, f32[528,3,9]{0,2,1:T(8,128)S(1)}, u32[]{:S(2)}, u32[]{:S(2)}) collective-permute-start(f32[528,3,9]{0,2,1:T(8,128)S(1)} %get-tuple-element.127), channel_id=1, source_target_pairs={{0,8},{8,16},{16,24},{1,9},{9,17},{17,25},{2,10},{10,18},{18,26},{... | collective-permute-start | bytes 171080 | tf_op jit(solution)/shard_map/ppermute | solution.py:209
  160.6 6.1 %collective-permute-start.8 = (f32[528,3,9]{0,2,1:T(8,128)S(1)}, f32[528,3,9]{0,2,1:T(8,128)S(1)}, u32[]{:S(2)}, u32[]{:S(2)}) collective-permute-start(f32[528,3,9]{0,2,1:T(8,128)S(1)} %get-tuple-element.126), channel_id=1, source_target_pairs={{8,0},{16,8},{24,16},{9,1},{17,9},{25,17},{10,2},{18,10},{26,18},{... | collective-permute-start | bytes 171080 | tf_op jit(solution)/shard_map/ppermute | solution.py:209
  166.7 7.5 %collective-permute-start.11 = (f32[9,3,24]{0,2,1:T(8,128)S(1)}, f32[9,3,24]{0,2,1:T(8,128)S(1)}, u32[]{:S(2)}, u32[]{:S(2)}) collective-permute-start(f32[9,3,24]{0,2,1:T(8,128)S(1)} %get-tuple-element.125), channel_id=1, source_target_pairs={{0,1},{1,2},{2,3},{3,4},{4,5},{5,6},{6,7},{8,9},{9,10},{10,11},{11... | collective-permute-start | bytes 7784 | tf_op jit(solution)/shard_map/ppermute | solution.py:209
  171.5 5.9 %collective-permute-start.10 = (f32[9,3,24]{0,2,1:T(8,128)S(1)}, f32[9,3,24]{0,2,1:T(8,128)S(1)}, u32[]{:S(2)}, u32[]{:S(2)}) collective-permute-start(f32[9,3,24]{0,2,1:T(8,128)S(1)} %get-tuple-element.124), channel_id=1, source_target_pairs={{1,0},{2,1},{3,2},{4,3},{5,4},{6,5},{7,6},{9,8},{10,9},{11,10},{12... | collective-permute-start | bytes 7784 | tf_op jit(solution)/shard_map/ppermute | solution.py:209
  174.2 11.7 %copy-start.15 = (f32[1,5,1,5,2,2,128]{6,5,4,2,1,3,0:T(2,128)S(1)}, f32[1,5,1,5,2,2,128]{6,5,4,2,1,3,0:T(2,128)}, u32[]{:S(2)}) copy-start(f32[1,5,1,5,2,2,128]{6,5,4,2,1,3,0:T(2,128)} %copy-done.14) | copy-start | bytes 153604
  174.2 11.7 %copy-start.17 = (f32[1,5,1,5,2,2,128]{6,5,4,2,1,3,0:T(2,128)S(1)}, f32[1,5,1,5,2,2,128]{6,5,4,2,1,3,0:T(2,128)}, u32[]{:S(2)}) copy-start(f32[1,5,1,5,2,2,128]{6,5,4,2,1,3,0:T(2,128)} %copy-done.16) | copy-start | bytes 153604
  180.7 5.2 %copy-start.21 = (f32[1,5,3,5,2,2,128]{6,5,4,1,3,2,0:T(2,128)S(1)}, f32[1,5,3,5,2,2,128]{6,5,4,1,3,2,0:T(2,128)}, u32[]{:S(2)}) copy-start(f32[1,5,3,5,2,2,128]{6,5,4,1,3,2,0:T(2,128)} %pad_maximum_fusion.15) | copy-start | bytes 460804
  189.5 7.8 %copy-start.32 = (f32[2,2,128]{2,1,0:T(2,128)S(1)}, f32[2,2,128]{2,1,0:T(2,128)}, u32[]{:S(2)}) copy-start(f32[2,2,128]{2,1,0:T(2,128)} %param.58) | copy-start | bytes 6148
  189.5 7.8 %copy-start.34 = (f32[2,2,128]{2,1,0:T(2,128)S(1)}, f32[2,2,128]{2,1,0:T(2,128)}, u32[]{:S(2)}) copy-start(f32[2,2,128]{2,1,0:T(2,128)} %param.57) | copy-start | bytes 6148
  206.8 9.0 %copy-start.22 = (f32[1,5,5,1,2,2,128]{6,5,4,2,1,3,0:T(2,128)S(1)}, f32[1,5,5,1,2,2,128]{6,5,4,2,1,3,0:T(2,128)}, u32[]{:S(2)}) copy-start(f32[1,5,5,1,2,2,128]{6,5,4,2,1,3,0:T(2,128)} %add_bitcast_fusion.4) | copy-start | bytes 153604
  206.8 9.0 %copy-start.23 = (f32[1,5,5,1,2,2,128]{6,5,4,2,1,3,0:T(2,128)S(1)}, f32[1,5,5,1,2,2,128]{6,5,4,2,1,3,0:T(2,128)}, u32[]{:S(2)}) copy-start(f32[1,5,5,1,2,2,128]{6,5,4,2,1,3,0:T(2,128)} %get-tuple-element.63) | copy-start | bytes 153604
  207.9 5.7 %collective-permute-start.16 = (f32[3,5,5,2,1,128]{5,3,0,2,1,4:T(2,128)S(1)}, f32[3,5,5,2,1,128]{5,3,0,2,1,4:T(2,128)S(1)}, u32[]{:S(2)}, u32[]{:S(2)}) collective-permute-start(f32[3,5,5,2,1,128]{5,3,0,2,1,4:T(2,128)S(1)} %get-tuple-element.128), channel_id=1, source_target_pairs={{0,8},{8,16},{16,24},{1,9},{9,17},{17,25},{2,10},{10,18},{18,26},{... | collective-permute-start | bytes 230408 | tf_op jit(solution)/shard_map/ppermute | solution.py:217
  213.9 4.2 %collective-permute-start.17 = (f32[3,5,5,2,1,128]{5,3,0,2,1,4:T(2,128)S(1)}, f32[3,5,5,2,1,128]{5,3,0,2,1,4:T(2,128)S(1)}, u32[]{:S(2)}, u32[]{:S(2)}) collective-permute-start(f32[3,5,5,2,1,128]{5,3,0,2,1,4:T(2,128)S(1)} %get-tuple-element.131), channel_id=1, source_target_pairs={{8,0},{16,8},{24,16},{9,1},{17,9},{25,17},{10,2},{18,10},{26,18},{... | collective-permute-start | bytes 230408 | tf_op jit(solution)/shard_map/ppermute | solution.py:218
  218.7 9.2 %collective-permute-start.18 = (f32[3,5,5,2,2,1]{5,4,3,1,0,2:T(2,128)S(1)}, f32[3,5,5,2,2,1]{5,4,3,1,0,2:T(2,128)S(1)}, u32[]{:S(2)}, u32[]{:S(2)}) collective-permute-start(f32[3,5,5,2,2,1]{5,4,3,1,0,2:T(2,128)S(1)} %slice.966), channel_id=1, source_target_pairs={{0,1},{1,2},{2,3},{3,4},{4,5},{5,6},{6,7},{8,9},{9,10},{10,11},{11... | collective-permute-start | bytes 3608 | tf_op jit(solution)/shard_map/ppermute | solution.py:217
  229.1 11.8 %copy-start.4 = (f32[3,5,5,5,2,2,128]{6,5,4,3,2,1,0:T(2,128)S(1)}, f32[3,5,5,5,2,2,128]{6,5,4,3,2,1,0:T(2,128)}, u32[]{:S(2)}) copy-start(f32[3,5,5,5,2,2,128]{6,5,4,3,2,1,0:T(2,128)} %param.54) | copy-start | bytes 2304004
  229.1 11.8 %copy-start.6 = (f32[3,5,5,5,2,2,128]{6,5,4,3,2,1,0:T(2,128)S(1)}, f32[3,5,5,5,2,2,128]{6,5,4,3,2,1,0:T(2,128)}, u32[]{:S(2)}) copy-start(f32[3,5,5,5,2,2,128]{6,5,4,3,2,1,0:T(2,128)} %copy-done.5) | copy-start | bytes 2304004
  229.1 7.7 %collective-permute-start.19 = (f32[3,5,5,2,2,1]{5,4,3,1,0,2:T(2,128)S(1)}, f32[3,5,5,2,2,1]{5,4,3,1,0,2:T(2,128)}, u32[]{:S(2)}, u32[]{:S(2)}) collective-permute-start(f32[3,5,5,2,2,1]{5,4,3,1,0,2:T(2,128)S(1)} %bitcast.199), channel_id=1, source_target_pairs={{1,0},{2,1},{3,2},{4,3},{5,4},{6,5},{7,6},{9,8},{10,9},{11,10},{12... | collective-permute-start | bytes 3608 | tf_op jit(solution)/shard_map/ppermute | solution.py:218
  (8 other events, 9.9 us)
where the time goes:
time: 246 us; the launch traced here: 243 us
  other arithmetic  80.1 us (33%)
  starting transfers between devices  65.2 us (27%)
  waiting for transfers between devices  34.3 us (14%)
  local copies, waits for them, and re-layouts  33.3 us (14%)
  Pallas kernels  27.6 us (11%)
    reduce_sum x4, other arithmetic, along(): return jnp.sum(coefs * jnp.expand_dims(x, axis), axis=axis + 1)  32.4 us
    pallas_call x1, Pallas kernels, load_table(): pl.pallas_call(load_kernel, grid=(rows // ROW_BLOCK,), in_specs=[pl.Block...  27.6 us
    ppermute x6, starting transfers between devices, shift_faces(): lax.ppermute(lax.slice_in_dim(low_face, 0, 1, axis=dim), axis, backward)  26.4 us
    ppermute x6, waiting for transfers between devices, shift_faces(): lax.ppermute(lax.slice_in_dim(high_face, size - 1, size, axis=dim), axis,...  20.2 us
    ppermute x6, starting transfers between devices, shift_faces(): lax.ppermute(lax.slice_in_dim(high_face, size - 1, size, axis=dim), axis,...  14.7 us
    mul x4, other arithmetic, advance(): slope_x = 0.5 * (ahead_x - behind_x)  14.7 us
    ppermute x4, starting transfers between devices, shift_block(): return lax.ppermute(block, axis, pairs)  12.4 us
    ppermute x6, waiting for transfers between devices, shift_faces(): lax.ppermute(lax.slice_in_dim(low_face, 0, 1, axis=dim), axis, backward)  8.17 us
  transfers between devices with their start and end apart: 20, of which 12 were waited for; matrix products, arithmetic and copies ran while one was open for 17% of the time, Pallas kernels for 0%

commit v1 on v0

--- a/solution.py
+++ b/solution.py
@@ -337,11 +337,18 @@
         surface_load,
         ((0, 0), (0, 0), (0, 0), (0, 4), (0, layers - 1), (0, 0), (0, 0)),
     )
-    masses = assemble(density[None, None, None, None] * weights_cube()[None])
+    mass_parts = density[None, None, None, None] * weights_cube()[None]
+    masses = None
     current = displacement
     for counter in range(SOLID_STEPS):
-        force = assemble(internal_force(current, lame_first, shear_modulus)) + load_padded
-        acceleration = force / masses
+        force = internal_force(current, lame_first, shear_modulus)
+        if masses is None:
+            joined = assemble(jnp.concatenate([force, mass_parts], axis=0))
+            force = joined[:3]
+            masses = joined[3:]
+        else:
+            force = assemble(force)
+        acceleration = (force + load_padded) / masses
         advanced = 2.0 * current - previous + solid_dt * solid_dt * acceleration
         previous = current
         current = advanced

time: 246 us -> 222 us (0.902)
  starting transfers between devices: 65.2 us -> 43.6 us
  other arithmetic: 80.1 us -> 89.5 us
  local copies, waits for them, and re-layouts: 33.3 us -> 26.8 us
  waiting for transfers between devices: 34.3 us -> 28.4 us
    ppermute x6 -> x4, starting transfers between devices: 26.4 us -> 10.3 us  [shift_faces(): lax.ppermute(lax.slice_in_dim(low_face, 0, 1, axis=dim), axis, backward)]
    mul x4, other arithmetic: 14.7 us -> 26 us  [advance(): slope_x = 0.5 * (ahead_x - behind_x)]
    ppermute x6 -> x4, waiting for transfers between devices: 20.2 us -> 13.2 us  [shift_faces(): lax.ppermute(lax.slice_in_dim(high_face, size - 1, size, axis=dim), axis,...]
    ppermute x6 -> x4, starting transfers between devices: 14.7 us -> 9.29 us  [shift_faces(): lax.ppermute(lax.slice_in_dim(high_face, size - 1, size, axis=dim), axis,...]
    ppermute x6 -> x4, waiting for transfers between devices: 8.17 us -> 8.38 us  [shift_faces(): lax.ppermute(lax.slice_in_dim(low_face, 0, 1, axis=dim), axis, backward)]
  transfers between devices with their start and end apart: 20 -> 16, of which waited for: 12 -> 11; matrix products, arithmetic and copies ran while one was open for 17% -> 18% of each run, Pallas kernels for 0% -> 0%
where the time goes in v1:
time: 222 us; the launch traced here: 218 us
  other arithmetic  89.5 us (40%)
  starting transfers between devices  43.6 us (20%)
  waiting for transfers between devices  28.4 us (13%)
  Pallas kernels  27.6 us (12%)
  local copies, waits for them, and re-layouts  26.8 us (12%)
    reduce_sum x4, other arithmetic, along(): return jnp.sum(coefs * jnp.expand_dims(x, axis), axis=axis + 1)  32.1 us
    pallas_call x1, Pallas kernels, load_table(): pl.pallas_call(load_kernel, grid=(rows // ROW_BLOCK,), in_specs=[pl.Block...  27.6 us
    mul x4, other arithmetic, advance(): slope_x = 0.5 * (ahead_x - behind_x)  26 us
    ppermute x4, waiting for transfers between devices, shift_faces(): lax.ppermute(lax.slice_in_dim(high_face, size - 1, size, axis=dim), axis,...  13.2 us
    ppermute x4, starting transfers between devices, shift_block(): return lax.ppermute(block, axis, pairs)  12.3 us
    ppermute x4, starting transfers between devices, shift_faces(): lax.ppermute(lax.slice_in_dim(low_face, 0, 1, axis=dim), axis, backward)  10.3 us
    ppermute x4, starting transfers between devices, shift_faces(): lax.ppermute(lax.slice_in_dim(high_face, size - 1, size, axis=dim), axis,...  9.29 us
    ppermute x4, waiting for transfers between devices, shift_faces(): lax.ppermute(lax.slice_in_dim(low_face, 0, 1, axis=dim), axis, backward)  8.38 us
  transfers between devices with their start and end apart: 16, of which 11 were waited for; matrix products, arithmetic and copies ran while one was open for 18% of the time, Pallas kernels for 0%

profile of v1, /device:TPU:10, one launch (start us, length us, event | category | flops | bytes accessed | tf_op | source)
XLA Modules:
  0.0 218.0 jit_solution(15711854853993399446)
XLA Ops:
  1.7 2.2 %pad_maximum_fusion.12 = (f32[8,4,2048]{2,1,0:T(4,128)}, f32[8,4,2048]{2,1,0:T(4,128)}) fusion(f32[1,32,2048]{2,1,0:T(8,128)} %bitcast.156, f32[1,32,2048]{2,1,0:T(8,128)S(1)} %fusion.124, f32[6,32,2048]{2,1,0:T(8,128)} %param.49), kind=kLoop, calls=%fused_computation.284 | loop fusion | flops 262144 | bytes 2621440 | tf_op jit(solution)/shard_map/slice | solution.py:35
  3.9 1.9 collective-permute-start.1
  5.8 3.1 %collective-permute-start = (f32[8,4,2048]{2,1,0:T(4,128)}, f32[8,4,2048]{2,1,0:T(4,128)}, u32[]{:S(2)}, u32[]{:S(2)}) collective-permute-start(f32[8,4,2048]{2,1,0:T(4,128)} %get-tuple-element.85), channel_id=1, source_target_pairs={{0,8},{8,16},{16,24},{1,9},{9,17},{17,25},{2,10},{10,18},{18,26},{... | collective-permute-start | bytes 786440 | tf_op jit(solution)/shard_map/ppermute | solution.py:34
  9.5 8.0 %multiply_reduce_fusion.30 = (f32[5,5,5,2,2,128]{5,4,3,2,1,0:T(2,128)S(1)}, f32[5,5,5,2,2,128]{5,4,3,2,1,0:T(2,128)S(1)}, f32[5,5,5,2,2,128]{5,4,3,2,1,0:T(2,128...) fusion(f32[5,5,5,2,2,128]{5,4,3,2,1,0:T(2,128)S(1)} %get-tuple-, ...), kind=kLoop, calls=%fused_computation.65 | loop fusion | flops 5184000 | bytes 3072100 | tf_op jit(solution)/shard_map/reduce_sum | solution.py:184
  18.5 8.1 %multiply_reduce_fusion.29 = (f32[5,5,5,2,2,128]{5,4,3,2,1,0:T(2,128)S(1)}, f32[5,5,5,2,2,128]{5,4,3,2,1,0:T(2,128)S(1)}, f32[5,5,5,2,2,128]{5,4,3,2,1,0:T(2,128...) fusion(f32[5,5,5,2,2,128]{5,4,3,2,1,0:T(2,128)S(1)} %get-tuple-, ...), kind=kLoop, calls=%fused_computation.64 | loop fusion | flops 5184000 | bytes 3840100 | tf_op jit(solution)/shard_map/reduce_sum | solution.py:184
  27.5 2.9 %collective-permute-start.5 = (f32[4,5,5,2,1,128]{5,3,2,1,0,4:T(2,128)S(1)}, f32[4,5,5,2,1,128]{5,3,2,1,0,4:T(2,128)S(1)}, u32[]{:S(2)}, u32[]{:S(2)}) collective-permute-start(f32[4,5,5,2,1,128]{5,3,2,1,0,4:T(2,128)S(1)} %get-tuple-element.116), channel_id=1, source_target_pairs={{8,0},{16,8},{24,16},{9,1},{17,9},{25,17},{10,2},{18,10},{26,18},{... | collective-permute-start | bytes 307208 | tf_op jit(solution)/shard_map/ppermute | solution.py:218
  32.7 1.9 collective-permute-start.4
  34.6 1.4 fusion.117
  36.0 2.8 %collective-permute-done.4 = f32[4,5,5,2,1,128]{5,3,2,1,0,4:T(2,128)S(1)} collective-permute-done((f32[4,5,5,2,1,128]{5,3,2,1,0,4:T(2,128)S(1)}, f32[4,5,5,2,1,128]{5,3,2,1,0,4:T(2,128)S(1)}, u32[]{:S(2)}, u32[]{:S(2)}) %collective-permute-start.4) | collective-permute-done | bytes 102432 | tf_op jit(solution)/shard_map/ppermute | solution.py:217
  40.7 3.3 %collective-permute-start.7 = (f32[4,5,5,2,2,1]{5,4,3,2,1,0:T(2,128)S(1)}, f32[4,5,5,2,2,1]{5,4,3,2,1,0:T(2,128)S(1)}, u32[]{:S(2)}, u32[]{:S(2)}) collective-permute-start(f32[4,5,5,2,2,1]{5,4,3,2,1,0:T(2,128)S(1)} %bitcast.159), channel_id=1, source_target_pairs={{1,0},{2,1},{3,2},{4,3},{5,4},{6,5},{7,6},{9,8},{10,9},{11,10},{12... | collective-permute-start | bytes 4808 | tf_op jit(solution)/shard_map/ppermute | solution.py:218
  44.9 2.5 %collective-permute-start.6 = (f32[4,5,5,2,2,1]{5,4,3,2,1,0:T(2,128)}, f32[4,5,5,2,2,1]{5,4,3,2,1,0:T(2,128)}, u32[]{:S(2)}, u32[]{:S(2)}) collective-permute-start(f32[4,5,5,2,2,1]{5,4,3,2,1,0:T(2,128)} %slice.854), channel_id=1, source_target_pairs={{0,1},{1,2},{2,3},{3,4},{4,5},{5,6},{6,7},{8,9},{9,10},{10,11},{11... | collective-permute-start | bytes 4808 | tf_op jit(solution)/shard_map/ppermute | solution.py:217
  48.4 2.1 collective-permute-done.7
  51.1 1.3 copy.199
  52.4 1.4 collective-permute-done.6
  53.8 1.5 copy.196
  55.3 1.3 copy.197
  56.6 1.4 maximum_add_fusion.3
  58.0 1.4 fusion.125
  60.5 1.4 pad_maximum_fusion.4
  62.0 1.9 collective-permute-start.2
  63.9 4.8 %collective-permute-start.3 = (f32[8,40,4]{2,1,0:T(8,128)S(1)}, f32[8,40,4]{2,1,0:T(8,128)}, u32[]{:S(2)}, u32[]{:S(2)}) collective-permute-start(f32[8,40,4]{2,1,0:T(8,128)S(1)} %get-tuple-element.81), channel_id=1, source_target_pairs={{1,0},{2,1},{3,2},{4,3},{5,4},{6,5},{7,6},{9,8},{10,9},{11,10},{12... | collective-permute-start | bytes 15368 | tf_op jit(solution)/shard_map/ppermute | solution.py:37
  70.8 1.5 collective-permute-done.3
  72.3 3.2 %concatenate.126 = f32[8,40,2056]{2,1,0:T(8,128)S(1)} concatenate(f32[8,40,4]{2,1,0:T(8,128)} %copy-done.19, f32[8,40,2048]{2,1,0:T(8,128)} %copy-done, f32[8,40,4]{2,1,0:T(8,128)} %collective-permute-done.3), dimensions={2} | concatenate | bytes 5263360 | tf_op jit(solution)/shard_map/concatenate | solution.py:38
  75.9 3.6 %subtract_multiply_fusion.7 = (f32[8,40,2056]{2,1,0:T(8,128)S(1)}, f32[8,40,2056]{2,1,0:T(8,128)S(1)}, f32[8,40,2056]{2,1,0:T(8,128)S(1)}) fusion(f32[8,40,2056]{2,1,0:T(8,128)S(1)} %pad_maximum_fusion), kind=kLoop, calls=%fused_computation.31 | loop fusion | flops 5921280 | bytes 10526720 | tf_op jit(solution)/shard_map/mul | solution.py:75
  81.4 3.6 %subtract_multiply_fusion.5 = (f32[8,40,2056]{2,1,0:T(8,128)S(1)}, f32[8,40,2056]{2,1,0:T(8,128)S(1)}, f32[8,40,2056]{2,1,0:T(8,128)S(1)}) fusion(f32[8,40,2056]{2,1,0:T(8,128)S(1)} %pad_maximum_fusion.1), kind=kLoop, calls=%fused_computation.28 | loop fusion | flops 5921280 | bytes 10526720 | tf_op jit(solution)/shard_map/mul | solution.py:75
  86.4 3.6 %subtract_multiply_fusion.3 = (f32[8,40,2056]{2,1,0:T(8,128)S(1)}, f32[8,40,2056]{2,1,0:T(8,128)S(1)}, f32[8,40,2056]{2,1,0:T(8,128)S(1)}) fusion(f32[8,40,2056]{2,1,0:T(8,128)S(1)} %pad_maximum_fusion.2), kind=kLoop, calls=%fused_computation.25 | loop fusion | flops 5921280 | bytes 10526720 | tf_op jit(solution)/shard_map/mul | solution.py:75
  91.5 15.3 %subtract_multiply_fusion.1 = (f32[8,40,2056]{2,1,0:T(8,128)S(1)}, f32[8,40,2056]{2,1,0:T(8,128)S(1)}, f32[8,40,2056]{2,1,0:T(8,128)S(1)}) fusion(f32[8,40,2056]{2,1,0:T(8,128)S(1)} %pad_maximum_fusion.3), kind=kLoop, calls=%fused_computation.22 | loop fusion | flops 5921280 | bytes 10526720 | tf_op jit(solution)/shard_map/mul | solution.py:75
  110.1 27.6 %shard_map.472 = f32[528,144]{1,0:T(8,128)} custom-call(f32[3,32,2048]{2,1,0:T(8,128)} %pad_maximum_fusion.5.trac_ref, s32[32,2048]{1,0:T(8,128)} %get-tuple-element.112.row_ref, s32[32,2048]{1,0:T(8,128)} %get-tuple-element.111.col_ref), custom_call_target="tpu_custom_call" | custom-call | tf_op jit(solution)/shard_map/pallas_call | solution.py:164
  139.0 1.9 collective-permute-start.9
  141.0 3.6 %collective-permute-start.8 = (f32[528,3,9]{0,2,1:T(8,128)S(1)}, f32[528,3,9]{0,2,1:T(8,128)S(1)}, u32[]{:S(2)}, u32[]{:S(2)}) collective-permute-start(f32[528,3,9]{0,2,1:T(8,128)S(1)} %get-tuple-element.123), channel_id=1, source_target_pairs={{8,0},{16,8},{24,16},{9,1},{17,9},{25,17},{10,2},{18,10},{26,18},{... | collective-permute-start | bytes 171080 | tf_op jit(solution)/shard_map/ppermute | solution.py:209
  144.6 1.5 fusion.1
  147.1 4.8 %collective-permute-start.11 = (f32[9,3,24]{0,2,1:T(8,128)S(1)}, f32[9,3,24]{0,2,1:T(8,128)S(1)}, u32[]{:S(2)}, u32[]{:S(2)}) collective-permute-start(f32[9,3,24]{0,2,1:T(8,128)S(1)} %get-tuple-element.122), channel_id=1, source_target_pairs={{0,1},{1,2},{2,3},{3,4},{4,5},{5,6},{6,7},{8,9},{9,10},{10,11},{11... | collective-permute-start | bytes 7784 | tf_op jit(solution)/shard_map/ppermute | solution.py:209
  151.9 1.9 collective-permute-start.10
  153.9 3.9 %collective-permute-done.10 = f32[9,3,24]{0,2,1:T(8,128)S(1)} collective-permute-done((f32[9,3,24]{0,2,1:T(8,128)S(1)}, f32[9,3,24]{0,2,1:T(8,128)S(1)}, u32[]{:S(2)}, u32[]{:S(2)}) %collective-permute-start.10) | collective-permute-done | bytes 2624 | tf_op jit(solution)/shard_map/ppermute | solution.py:209
  159.1 1.3 slice.874
  161.6 1.4 copy.208
  163.1 2.3 %multiply_add_fusion.1 = f32[3,5,5,5,2,2,128]{6,5,4,3,2,1,0:T(2,128)S(1)} fusion(f32[3,5,5,5,2,2,128]{6,5,4,3,2,1,0:T(2,128)} %param.55, f32[3,5,5,5,2,2,128]{6,5,4,3,2,1,0:T(2,128)S(1)} %copy-done.3, f32[3,5,5,1,1,2,128]{6,5,4,3,2,1,0:T(2,128)S(1)} %maximum_bitcast_fusion.4, f32[4,5,5,5,2,2,128]{6,5,4,3,2,1,0:T(2,128)} %copy-done.7, ...), kind=kLoop, calls=%fused_computation.90 | loop fusion | flops 1152000 | bytes 3404800 | tf_op jit(solution)/shard_map/add | solution.py:352
  166.6 7.8 %multiply_reduce_fusion.4 = (f32[5,5,5,2,2,128]{5,4,3,2,1,0:T(2,128)S(1)}, f32[5,5,5,2,2,128]{5,4,3,2,1,0:T(2,128)S(1)}, f32[5,5,5,2,2,128]{5,4,3,2,1,0:T(2,128)...) fusion(f32[5,5,5,2,2,128]{5,4,3,2,1,0:T(2,128)S(1)} %get-tuple-, ...), kind=kLoop, calls=%fused_computation.39 | loop fusion | flops 5184000 | bytes 3072100 | tf_op jit(solution)/shard_map/reduce_sum | solution.py:184
  175.3 8.1 %multiply_reduce_fusion.1 = (f32[5,5,5,2,2,128]{5,4,3,2,1,0:T(2,128)S(1)}, f32[5,5,5,2,2,128]{5,4,3,2,1,0:T(2,128)S(1)}, f32[5,5,5,2,2,128]{5,4,3,2,1,0:T(2,128)...) fusion(f32[5,5,5,2,2,128]{5,4,3,2,1,0:T(2,128)S(1)} %get-tuple-, ...), kind=kLoop, calls=%fused_computation.36 | loop fusion | flops 5184000 | bytes 3840100 | tf_op jit(solution)/shard_map/reduce_sum | solution.py:184
  184.8 1.9 collective-permute-start.12
  186.7 3.8 %collective-permute-done.12 = f32[3,5,5,2,1,128]{5,3,0,2,1,4:T(2,128)S(1)} collective-permute-done((f32[3,5,5,2,1,128]{5,3,0,2,1,4:T(2,128)S(1)}, f32[3,5,5,2,1,128]{5,3,0,2,1,4:T(2,128)S(1)}, u32[]{:S(2)}, u32[]{:S(2)}) %collective-permute-start.12) | collective-permute-done | bytes 76832 | tf_op jit(solution)/shard_map/ppermute | solution.py:217
  190.7 2.1 collective-permute-start.13
  192.8 1.6 slice.847
  195.5 2.9 %collective-permute-start.14 = (f32[3,5,5,2,2,1]{5,4,3,1,0,2:T(2,128)S(1)}, f32[3,5,5,2,2,1]{5,4,3,1,0,2:T(2,128)S(1)}, u32[]{:S(2)}, u32[]{:S(2)}) collective-permute-start(f32[3,5,5,2,2,1]{5,4,3,1,0,2:T(2,128)S(1)} %slice.887), channel_id=1, source_target_pairs={{0,1},{1,2},{2,3},{3,4},{4,5},{5,6},{6,7},{8,9},{9,10},{10,11},{11... | collective-permute-start | bytes 3608 | tf_op jit(solution)/shard_map/ppermute | solution.py:217
  199.4 5.3 %collective-permute-done.14 = f32[3,5,5,2,2,1]{5,4,3,1,0,2:T(2,128)S(1)} collective-permute-done((f32[3,5,5,2,2,1]{5,4,3,1,0,2:T(2,128)S(1)}, f32[3,5,5,2,2,1]{5,4,3,1,0,2:T(2,128)S(1)}, u32[]{:S(2)}, u32[]{:S(2)}) %collective-permute-start.14) | collective-permute-done | bytes 1232 | tf_op jit(solution)/shard_map/ppermute | solution.py:217
  205.9 2.1 collective-permute-start.15
  208.2 5.3 %collective-permute-done.15 = f32[3,5,5,2,2,1]{5,4,3,1,0,2:T(2,128)S(1)} collective-permute-done((f32[3,5,5,2,2,1]{5,4,3,1,0,2:T(2,128)S(1)}, f32[3,5,5,2,2,1]{5,4,3,1,0,2:T(2,128)S(1)}, u32[]{:S(2)}, u32[]{:S(2)}) %collective-permute-start.15) | collective-permute-done | bytes 1232 | tf_op jit(solution)/shard_map/ppermute | solution.py:218
  215.1 2.7 %multiply_add_fusion = f32[3,5,5,5,2,2,128]{6,5,4,3,2,1,0:T(2,128)} fusion(f32[3,5,5,5,2,2,128]{6,5,4,3,2,1,0:T(2,128)S(1)} %copy-done.3, f32[3,5,5,5,2,2,128]{6,5,4,3,2,1,0:T(2,128)S(1)} %copy-done.5, f32[3,5,5,1,1,2,128]{6,5,4,3,2,1,0:T(2,128)S(1)} %maximum_bitcast_fusion.4, f32[3,5,5,1,2,2,128]{6,5,4,3,2,1,0:T(2,128)S(1)} %add_bitcast_fusion.2, ...), kind=kLoop, calls=%fused_computation.89 | loop fusion | flops 1766400 | bytes 3712000 | tf_op jit(solution)/shard_map/add | solution.py:352
  (175 shorter events, 35.0 us)
Async XLA Ops:
  0.6 8.6 %copy-start.18 = (f32[5,5,5]{2,1,0:T(8,128)S(1)}, f32[5,5,5]{2,1,0:T(8,128)}, u32[]{:S(2)}) copy-start(f32[5,5,5]{2,1,0:T(8,128)} %constant.155) | copy-start | bytes 1504
  0.6 8.8 %copy-start.21 = (f32[5,5]{1,0:T(8,128)S(1)}, f32[5,5]{1,0:T(8,128)}, u32[]{:S(2)}) copy-start(f32[5,5]{1,0:T(8,128)} %constant.156) | copy-start | bytes 304
  0.7 8.3 %copy-start.2 = (f32[3,5,5,5,2,2,128]{6,5,4,3,2,1,0:T(2,128)S(1)}, f32[3,5,5,5,2,2,128]{6,5,4,3,2,1,0:T(2,128)}, u32[]{:S(2)}) copy-start(f32[3,5,5,5,2,2,128]{6,5,4,3,2,1,0:T(2,128)} %param.54) | copy-start | bytes 2304004
  0.7 8.6 %copy-start.24 = (f32[2,2,128]{2,1,0:T(2,128)S(1)}, f32[2,2,128]{2,1,0:T(2,128)}, u32[]{:S(2)}) copy-start(f32[2,2,128]{2,1,0:T(2,128)} %param.56) | copy-start | bytes 6148
  1.7 7.5 %copy-start.13 = (f32[1,32,2048]{2,1,0:T(8,128)}, f32[1,32,2048]{2,1,0:T(8,128)S(1)}, u32[]{:S(2)}) copy-start(f32[1,32,2048]{2,1,0:T(8,128)S(1)} %fusion.124) | copy-start | bytes 786436
  3.9 56.5 %collective-permute-start.1 = (f32[8,4,2048]{2,1,0:T(4,128)}, f32[8,4,2048]{2,1,0:T(4,128)}, u32[]{:S(2)}, u32[]{:S(2)}) collective-permute-start(f32[8,4,2048]{2,1,0:T(4,128)} %get-tuple-element.86), channel_id=1, source_target_pairs={{8,0},{16,8},{24,16},{9,1},{17,9},{25,17},{10,2},{18,10},{26,18},{... | collective-permute-start | bytes 786440 | tf_op jit(solution)/shard_map/ppermute | solution.py:37
  5.8 54.6 %collective-permute-start = (f32[8,4,2048]{2,1,0:T(4,128)}, f32[8,4,2048]{2,1,0:T(4,128)}, u32[]{:S(2)}, u32[]{:S(2)}) collective-permute-start(f32[8,4,2048]{2,1,0:T(4,128)} %get-tuple-element.85), channel_id=1, source_target_pairs={{0,8},{8,16},{16,24},{1,9},{9,17},{17,25},{2,10},{10,18},{18,26},{... | collective-permute-start | bytes 786440 | tf_op jit(solution)/shard_map/ppermute | solution.py:34
  9.2 8.3 %copy-start.22 = (f32[2,2,128]{2,1,0:T(2,128)S(1)}, f32[2,2,128]{2,1,0:T(2,128)}, u32[]{:S(2)}) copy-start(f32[2,2,128]{2,1,0:T(2,128)} %param.58) | copy-start | bytes 6148
  9.3 8.3 %copy-start.23 = (f32[2,2,128]{2,1,0:T(2,128)S(1)}, f32[2,2,128]{2,1,0:T(2,128)}, u32[]{:S(2)}) copy-start(f32[2,2,128]{2,1,0:T(2,128)} %param.57) | copy-start | bytes 6148
  17.5 0.9 copy-start.20
  27.3 7.4 %copy-start.16 = (s32[32,2048]{1,0:T(8,128)S(1)}, s32[32,2048]{1,0:T(8,128)}, u32[]{:S(2)}) copy-start(s32[32,2048]{1,0:T(8,128)} %param.53) | copy-start | bytes 786436
  27.3 7.4 %copy-start.17 = (s32[32,2048]{1,0:T(8,128)S(1)}, s32[32,2048]{1,0:T(8,128)}, u32[]{:S(2)}) copy-start(s32[32,2048]{1,0:T(8,128)} %param.52) | copy-start | bytes 786436
  27.5 4.7 %collective-permute-start.5 = (f32[4,5,5,2,1,128]{5,3,2,1,0,4:T(2,128)S(1)}, f32[4,5,5,2,1,128]{5,3,2,1,0,4:T(2,128)S(1)}, u32[]{:S(2)}, u32[]{:S(2)}) collective-permute-start(f32[4,5,5,2,1,128]{5,3,2,1,0,4:T(2,128)S(1)} %get-tuple-element.116), channel_id=1, source_target_pairs={{8,0},{16,8},{24,16},{9,1},{17,9},{25,17},{10,2},{18,10},{26,18},{... | collective-permute-start | bytes 307208 | tf_op jit(solution)/shard_map/ppermute | solution.py:218
  32.7 6.1 %collective-permute-start.4 = (f32[4,5,5,2,1,128]{5,3,2,1,0,4:T(2,128)S(1)}, f32[4,5,5,2,1,128]{5,3,2,1,0,4:T(2,128)S(1)}, u32[]{:S(2)}, u32[]{:S(2)}) collective-permute-start(f32[4,5,5,2,1,128]{5,3,2,1,0,4:T(2,128)S(1)} %get-tuple-element.113), channel_id=1, source_target_pairs={{0,8},{8,16},{16,24},{1,9},{9,17},{17,25},{2,10},{10,18},{18,26},{... | collective-permute-start | bytes 307208 | tf_op jit(solution)/shard_map/ppermute | solution.py:217
  40.7 9.8 %collective-permute-start.7 = (f32[4,5,5,2,2,1]{5,4,3,2,1,0:T(2,128)S(1)}, f32[4,5,5,2,2,1]{5,4,3,2,1,0:T(2,128)S(1)}, u32[]{:S(2)}, u32[]{:S(2)}) collective-permute-start(f32[4,5,5,2,2,1]{5,4,3,2,1,0:T(2,128)S(1)} %bitcast.159), channel_id=1, source_target_pairs={{1,0},{2,1},{3,2},{4,3},{5,4},{6,5},{7,6},{9,8},{10,9},{11,10},{12... | collective-permute-start | bytes 4808 | tf_op jit(solution)/shard_map/ppermute | solution.py:218
  44.9 8.9 %collective-permute-start.6 = (f32[4,5,5,2,2,1]{5,4,3,2,1,0:T(2,128)}, f32[4,5,5,2,2,1]{5,4,3,2,1,0:T(2,128)}, u32[]{:S(2)}, u32[]{:S(2)}) collective-permute-start(f32[4,5,5,2,2,1]{5,4,3,2,1,0:T(2,128)} %slice.854), channel_id=1, source_target_pairs={{0,1},{1,2},{2,3},{3,4},{4,5},{5,6},{6,7},{8,9},{9,10},{10,11},{11... | collective-permute-start | bytes 4808 | tf_op jit(solution)/shard_map/ppermute | solution.py:217
  52.4 8.0 %copy-start.6 = (f32[6,32,2048]{2,1,0:T(8,128)S(1)}, f32[6,32,2048]{2,1,0:T(8,128)}, u32[]{:S(2)}) copy-start(f32[6,32,2048]{2,1,0:T(8,128)} %param.49) | copy-start | bytes 4718596
  52.4 8.1 %copy-start.11 = (f32[32,2048]{1,0:T(8,128)S(1)}, f32[32,2048]{1,0:T(8,128)}, u32[]{:S(2)}) copy-start(f32[32,2048]{1,0:T(8,128)} %param.50) | copy-start | bytes 786436
  56.6 3.9 %copy-start.14 = (f32[1,32,2048]{2,1,0:T(8,128)S(1)}, f32[1,32,2048]{2,1,0:T(8,128)}, u32[]{:S(2)}) copy-start(f32[1,32,2048]{2,1,0:T(8,128)} %copy-done.13) | copy-start | bytes 786436
  58.0 2.4 %copy-start.8 = (f32[4,5,1,5,2,2,128]{6,5,4,3,2,1,0:T(2,128)}, f32[4,5,1,5,2,2,128]{6,5,4,3,2,1,0:T(2,128)S(1)}, u32[]{:S(2)}) copy-start(f32[4,5,1,5,2,2,128]{6,5,4,3,2,1,0:T(2,128)S(1)} %maximum_add_fusion.3) | copy-start | bytes 614404
  59.4 1.0 copy-start.10
  61.9 8.2 %copy-start = (f32[8,40,2048]{2,1,0:T(8,128)}, f32[8,40,2048]{2,1,0:T(8,128)S(1)}, u32[]{:S(2)}) copy-start(f32[8,40,2048]{2,1,0:T(8,128)S(1)} %pad_maximum_fusion.4) | copy-start | bytes 7864324
  62.0 8.1 %collective-permute-start.2 = (f32[8,40,4]{2,1,0:T(8,128)S(1)}, f32[8,40,4]{2,1,0:T(8,128)S(1)}, u32[]{:S(2)}, u32[]{:S(2)}) collective-permute-start(f32[8,40,4]{2,1,0:T(8,128)S(1)} %get-tuple-element.82), channel_id=1, source_target_pairs={{0,1},{1,2},{2,3},{3,4},{4,5},{5,6},{6,7},{8,9},{9,10},{10,11},{11... | collective-permute-start | bytes 15368 | tf_op jit(solution)/shard_map/ppermute | solution.py:34
  63.9 8.3 %collective-permute-start.3 = (f32[8,40,4]{2,1,0:T(8,128)S(1)}, f32[8,40,4]{2,1,0:T(8,128)}, u32[]{:S(2)}, u32[]{:S(2)}) collective-permute-start(f32[8,40,4]{2,1,0:T(8,128)S(1)} %get-tuple-element.81), channel_id=1, source_target_pairs={{1,0},{2,1},{3,2},{4,3},{5,4},{6,5},{7,6},{9,8},{10,9},{11,10},{12... | collective-permute-start | bytes 15368 | tf_op jit(solution)/shard_map/ppermute | solution.py:37
  70.1 0.7 copy-start.19
  79.9 1.0 copy-start.1
  107.8 1.0 copy-start.12
  107.8 1.0 copy-start.15
  109.2 35.4 %copy-start.9 = (f32[4,5,1,5,2,2,128]{6,5,4,3,2,1,0:T(2,128)S(1)}, f32[4,5,1,5,2,2,128]{6,5,4,3,2,1,0:T(2,128)}, u32[]{:S(2)}) copy-start(f32[4,5,1,5,2,2,128]{6,5,4,3,2,1,0:T(2,128)} %copy-done.8) | copy-start | bytes 614404
  139.0 7.1 %collective-permute-start.9 = (f32[528,3,9]{0,2,1:T(8,128)S(1)}, f32[528,3,9]{0,2,1:T(8,128)S(1)}, u32[]{:S(2)}, u32[]{:S(2)}) collective-permute-start(f32[528,3,9]{0,2,1:T(8,128)S(1)} %get-tuple-element.124), channel_id=1, source_target_pairs={{0,8},{8,16},{16,24},{1,9},{9,17},{17,25},{2,10},{10,18},{18,26},{... | collective-permute-start | bytes 171080 | tf_op jit(solution)/shard_map/ppermute | solution.py:209
  141.0 6.1 %collective-permute-start.8 = (f32[528,3,9]{0,2,1:T(8,128)S(1)}, f32[528,3,9]{0,2,1:T(8,128)S(1)}, u32[]{:S(2)}, u32[]{:S(2)}) collective-permute-start(f32[528,3,9]{0,2,1:T(8,128)S(1)} %get-tuple-element.123), channel_id=1, source_target_pairs={{8,0},{16,8},{24,16},{9,1},{17,9},{25,17},{10,2},{18,10},{26,18},{... | collective-permute-start | bytes 171080 | tf_op jit(solution)/shard_map/ppermute | solution.py:209
  146.2 7.7 %copy-start.7 = (f32[4,5,5,5,2,2,128]{6,5,4,3,2,1,0:T(2,128)}, f32[4,5,5,5,2,2,128]{6,5,4,3,2,1,0:T(2,128)S(1)}, u32[]{:S(2)}) copy-start(f32[4,5,5,5,2,2,128]{6,5,4,3,2,1,0:T(2,128)S(1)} %fusion.1) | copy-start | bytes 3072004
  147.1 6.8 %collective-permute-start.11 = (f32[9,3,24]{0,2,1:T(8,128)S(1)}, f32[9,3,24]{0,2,1:T(8,128)S(1)}, u32[]{:S(2)}, u32[]{:S(2)}) collective-permute-start(f32[9,3,24]{0,2,1:T(8,128)S(1)} %get-tuple-element.122), channel_id=1, source_target_pairs={{0,1},{1,2},{2,3},{3,4},{4,5},{5,6},{6,7},{8,9},{9,10},{10,11},{11... | collective-permute-start | bytes 7784 | tf_op jit(solution)/shard_map/ppermute | solution.py:209
  151.9 5.9 %collective-permute-start.10 = (f32[9,3,24]{0,2,1:T(8,128)S(1)}, f32[9,3,24]{0,2,1:T(8,128)S(1)}, u32[]{:S(2)}, u32[]{:S(2)}) collective-permute-start(f32[9,3,24]{0,2,1:T(8,128)S(1)} %get-tuple-element.121), channel_id=1, source_target_pairs={{1,0},{2,1},{3,2},{4,3},{5,4},{6,5},{7,6},{9,8},{10,9},{11,10},{12... | collective-permute-start | bytes 7784 | tf_op jit(solution)/shard_map/ppermute | solution.py:209
  153.9 9.2 %copy-start.3 = (f32[3,5,5,5,2,2,128]{6,5,4,3,2,1,0:T(2,128)S(1)}, f32[3,5,5,5,2,2,128]{6,5,4,3,2,1,0:T(2,128)}, u32[]{:S(2)}) copy-start(f32[3,5,5,5,2,2,128]{6,5,4,3,2,1,0:T(2,128)} %param.54) | copy-start | bytes 2304004
  165.4 0.9 copy-start.4
  184.8 5.7 %collective-permute-start.12 = (f32[3,5,5,2,1,128]{5,3,0,2,1,4:T(2,128)S(1)}, f32[3,5,5,2,1,128]{5,3,0,2,1,4:T(2,128)S(1)}, u32[]{:S(2)}, u32[]{:S(2)}) collective-permute-start(f32[3,5,5,2,1,128]{5,3,0,2,1,4:T(2,128)S(1)} %get-tuple-element.125), channel_id=1, source_target_pairs={{0,8},{8,16},{16,24},{1,9},{9,17},{17,25},{2,10},{10,18},{18,26},{... | collective-permute-start | bytes 230408 | tf_op jit(solution)/shard_map/ppermute | solution.py:217
  190.7 4.2 %collective-permute-start.13 = (f32[3,5,5,2,1,128]{5,3,0,2,1,4:T(2,128)S(1)}, f32[3,5,5,2,1,128]{5,3,0,2,1,4:T(2,128)S(1)}, u32[]{:S(2)}, u32[]{:S(2)}) collective-permute-start(f32[3,5,5,2,1,128]{5,3,0,2,1,4:T(2,128)S(1)} %get-tuple-element.128), channel_id=1, source_target_pairs={{8,0},{16,8},{24,16},{9,1},{17,9},{25,17},{10,2},{18,10},{26,18},{... | collective-permute-start | bytes 230408 | tf_op jit(solution)/shard_map/ppermute | solution.py:218
  195.5 9.2 %collective-permute-start.14 = (f32[3,5,5,2,2,1]{5,4,3,1,0,2:T(2,128)S(1)}, f32[3,5,5,2,2,1]{5,4,3,1,0,2:T(2,128)S(1)}, u32[]{:S(2)}, u32[]{:S(2)}) collective-permute-start(f32[3,5,5,2,2,1]{5,4,3,1,0,2:T(2,128)S(1)} %slice.887), channel_id=1, source_target_pairs={{0,1},{1,2},{2,3},{3,4},{4,5},{5,6},{6,7},{8,9},{9,10},{10,11},{11... | collective-permute-start | bytes 3608 | tf_op jit(solution)/shard_map/ppermute | solution.py:217
  205.9 9.2 %copy-start.5 = (f32[3,5,5,5,2,2,128]{6,5,4,3,2,1,0:T(2,128)S(1)}, f32[3,5,5,5,2,2,128]{6,5,4,3,2,1,0:T(2,128)}, u32[]{:S(2)}) copy-start(f32[3,5,5,5,2,2,128]{6,5,4,3,2,1,0:T(2,128)} %copy-done.4) | copy-start | bytes 2304004
  205.9 7.5 %collective-permute-start.15 = (f32[3,5,5,2,2,1]{5,4,3,1,0,2:T(2,128)S(1)}, f32[3,5,5,2,2,1]{5,4,3,1,0,2:T(2,128)S(1)}, u32[]{:S(2)}, u32[]{:S(2)}) collective-permute-start(f32[3,5,5,2,2,1]{5,4,3,1,0,2:T(2,128)S(1)} %bitcast.162), channel_id=1, source_target_pairs={{1,0},{2,1},{3,2},{4,3},{5,4},{6,5},{7,6},{9,8},{10,9},{11,10},{12... | collective-permute-start | bytes 3608 | tf_op jit(solution)/shard_map/ppermute | solution.py:218
